TPU v7x, 128 devices: a whole 4x4x4 slice. The times are simulated.
128 devices in a mesh: sec: 2 (over x_hi), head: 4 (over x_lo, core), ctx: 16 (over z, y).
Axes of the slice: x: 4 (x_hi: 2, x_lo: 2; x = x_hi * 2 + x_lo), y: 4, z: 4, core: 2. Of those that a mesh axis runs over, the one named last changes fastest.
Arguments:
- proposal_rows: bfloat16 [512, 8192], P('sec', 'ctx'), may hold values from -400 to 400
- norm_gain: bfloat16 [8192], P('ctx'), may hold values from 0.25 to 1.75
- query_weight: bfloat16 [8192, 8192], P('ctx', ('sec', 'head')), may hold values from -0.0625 to 0.0625
- key_weight: bfloat16 [8192, 8, 128], P('ctx', ('sec', 'head')), may hold values from -0.25 to 0.25
- value_weight: bfloat16 [8192, 8, 128], P('ctx', ('sec', 'head')), may hold values from -0.0625 to 0.0625
- out_weight: bfloat16 [8192, 8192], P(('sec', 'head'), 'ctx'), may hold values from -0.0625 to 0.0625
- context_keys: bfloat16 [32768, 8, 128], P('ctx', ('sec', 'head')), may hold values from -256 to 256
- context_values: bfloat16 [32768, 8, 128], P('ctx', ('sec', 'head')), may hold values from -5 to 5
- prefix_lengths: int32 [32], replicated, may hold values from 2048 to 32768, as said below
- parents: int32 [512], replicated, may hold values from -1 to 510, as said below
Outputs:
- block_output: bfloat16 [512, 8192], P(('sec', 'head'), 'ctx')
Inputs may be any that keep to these rules, and one draw needn't show every extreme that they name: `parents`: token i = 16 p + s of particle p has parent -1 when s = 0, else 16 q + s - 1 for some particle q <= p. `prefix_lengths`: some particle sees the whole context.
All inputs are finite; a program needn't handle non-finite values.
Results may differ from a plain program's by a relative error of at most 0.015.
The roundings to bfloat16 on the way count: a program that leaves them out, or rounds other values in their place, can miss the bound.
Values may be sent and summed in bfloat16 or wider, within the bound.
No kernel may reach another device: no remote copies, remote signals or barrier semaphores. Data moves between devices by JAX's collectives and lax.ppermute only.
A program may use at most 192 MiB of HBM per device.

v0:
```python
import math
import jax
import jax.numpy as jnp
from jax import lax
from jax.sharding import PartitionSpec as P

D = 8192
PROPOSALS = 16
NEGATIVE = -1e30
EPSILON = 1e-05


def ancestry_columns(parents, column_offset, column_amount):
    total = parents.shape[0]
    index = jnp.arange(total, dtype=jnp.int32)
    step = jnp.logical_or(parents[:, None] == index[None, :], index[:, None] == index[None, :])
    reach = step.astype(jnp.bfloat16)
    for _ in range(3):
        reach = (jnp.dot(reach, reach, preferred_element_type=jnp.float32) > 0).astype(jnp.bfloat16)
    columns = lax.dynamic_slice_in_dim(reach, column_offset, column_amount, 1)
    return jnp.dot(reach, columns, preferred_element_type=jnp.float32) > 0


def body(
    proposal_rows,
    norm_gain,
    query_weight,
    key_weight,
    value_weight,
    out_weight,
    context_keys,
    context_values,
    prefix_lengths,
    parents,
):
    gathered = lax.all_gather(proposal_rows, "sec", axis=0, tiled=True)
    gathered_wide = gathered.astype(jnp.float32)
    total_rows = gathered.shape[0]
    squares = jnp.sum(gathered_wide * gathered_wide, axis=1)
    scaled = (gathered_wide * norm_gain.astype(jnp.float32)[None, :]).astype(jnp.bfloat16)
    query_width = query_weight.shape[1]
    head_size = key_weight.shape[2]
    groups = query_width // head_size
    joined = jnp.concatenate([query_weight, key_weight[:, 0, :], value_weight[:, 0, :]], axis=1)
    partial_value = jnp.dot(scaled, joined, preferred_element_type=jnp.float32)
    proj_width = partial_value.shape[1]
    lane = jnp.arange(128, dtype=jnp.int32)
    square_block = jnp.where(lane[None, :] == 0, squares[:, None], 0.0)
    packed = jnp.concatenate([partial_value, square_block], axis=1)
    reduced = lax.psum_scatter(packed, "ctx", scatter_dimension=0, tiled=True)
    row_share = reduced.shape[0]
    inverse = lax.rsqrt(reduced[:, proj_width] / D + EPSILON)[:, None]
    settled = reduced[:, :proj_width] * inverse
    own_queries = settled[:, :query_width].astype(jnp.bfloat16)
    tree_keys = settled[:, query_width : query_width + head_size].astype(jnp.bfloat16)
    tree_vals = settled[:, query_width + head_size :].astype(jnp.bfloat16)
    queries = lax.all_gather(own_queries, "ctx", axis=0, tiled=True)
    position = lax.axis_index("ctx")
    keys = context_keys[:, 0, :]
    vals = context_values[:, 0, :]
    span = keys.shape[0]
    factor = 1.0 / math.sqrt(head_size)
    grouped = queries.reshape(total_rows, groups, head_size)
    lengths_rows = jnp.repeat(prefix_lengths, PROPOSALS)
    positions = position * span + jnp.arange(span, dtype=jnp.int32)
    visible = (positions[None, :] < lengths_rows[:, None])[:, None, :]
    scores = jnp.einsum("rgd,td->rgt", grouped, keys, preferred_element_type=jnp.float32) * factor
    tree_visible = ancestry_columns(parents, position * row_share, row_share)[:, None, :]
    tree_scores = (
        jnp.einsum("rgd,td->rgt", grouped, tree_keys, preferred_element_type=jnp.float32) * factor
    )
    local_high = jnp.maximum(
        jnp.max(jnp.where(visible, scores, NEGATIVE), axis=2),
        jnp.max(jnp.where(tree_visible, tree_scores, NEGATIVE), axis=2),
    )
    highest = lax.pmax(local_high, "ctx")
    weights = jnp.where(visible, jnp.exp(scores - highest[:, :, None]), 0.0)
    tree_weights = jnp.where(tree_visible, jnp.exp(tree_scores - highest[:, :, None]), 0.0)
    weight_sum = jnp.sum(weights, axis=2) + jnp.sum(tree_weights, axis=2)
    summed = jnp.einsum(
        "rgt,td->rgd", weights.astype(jnp.bfloat16), vals, preferred_element_type=jnp.float32
    ) + jnp.einsum(
        "rgt,td->rgd",
        tree_weights.astype(jnp.bfloat16),
        tree_vals,
        preferred_element_type=jnp.float32,
    )
    sum_block = jnp.concatenate(
        [weight_sum, jnp.zeros((total_rows, 128 - groups), jnp.float32)], axis=1
    )
    packed_attn = jnp.concatenate([summed.reshape(total_rows, query_width), sum_block], axis=1)
    merged = lax.psum_scatter(packed_attn, "ctx", scatter_dimension=0, tiled=True)
    own_attended = (
        (
            merged[:, :query_width].reshape(row_share, groups, head_size)
            / merged[:, query_width : query_width + groups][:, :, None]
        )
        .reshape(row_share, query_width)
        .astype(jnp.bfloat16)
    )
    attended = lax.all_gather(own_attended, "ctx", axis=0, tiled=True)
    return lax.psum_scatter(
        jnp.dot(attended, out_weight, preferred_element_type=jnp.float32).astype(jnp.bfloat16),
        ("sec", "head"),
        scatter_dimension=0,
        tiled=True,
    )


def solution(mesh):
    placed = (
        P("sec", "ctx"),
        P("ctx"),
        P("ctx", ("sec", "head")),
        P("ctx", ("sec", "head"), None),
        P("ctx", ("sec", "head"), None),
        P(("sec", "head"), "ctx"),
        P("ctx", ("sec", "head"), None),
        P("ctx", ("sec", "head"), None),
        P(),
        P(),
    )
    return jax.shard_map(
        body, mesh=mesh, in_specs=placed, out_specs=P(("sec", "head"), "ctx"), check_vma=False
    )
```

profile of v0, /device:TPU:0, one launch (start us, length us, event | category | flops | bytes accessed | tf_op | source)
XLA Modules:
  0.0 426.5 jit_solution(10706751456148544928)
XLA Ops:
  6.5 10.5 %all_gather.9 = bf16[512,512]{1,0:T(8,128)(2,1)S(1)} all-gather(bf16[256,512]{1,0:T(8,128)(2,1)} %param.10), channel_id=1, replica_groups=mesh['sec'=2,'head'=4,'ctx'=16] {'sec'}, dimensions={0}, use_global_device_ids=true | all-gather | bytes 786432 | tf_op jit(solution)/shard_map/all_gather | solution.py:36
  17.0 0.7 convert_element_type.29
  18.0 2.2 fusion.5
  20.3 1.8 pad_maximum_fusion
  22.1 79.1 %reduce-scatter.6.cloned.1.call-done = f32[32,1408]{1,0:T(8,128)} async-done(((f32[512,1408]{1,0:T(8,128)}), f32[32,1408]{1,0:T(8,128)}) %reduce-scatter.6.cloned.1.call-update) | async-done | bytes 180240 | tf_op jit(solution)/shard_map/reduce_scatter | solution.py:50
  101.3 0.8 fusion.37
  102.1 1.0 fusion.34
  104.7 1.1 convolution_compare_fusion
  106.3 0.7 broadcast_compare_fusion
  106.9 38.8 %all-gather.3.cloned.1.call-done = bf16[512,1024]{1,0:T(8,128)(2,1)} async-done(((bf16[32,1024]{1,0:T(8,128)(2,1)}), bf16[512,1024]{1,0:T(8,128)(2,1)}) %all-gather.3.cloned.1.call-update) | async-done | bytes 1048592 | tf_op jit(solution)/shard_map/all_gather | solution.py:57
  145.7 1.7 select_reduce_fusion.1
  147.4 15.1 %select_reduce_fusion = (f32[512,8]{0,1:T(8,128)S(1)}, f32[512,8,2048]{2,0,1:T(8,128)}) fusion(pred[512,2048]{1,0:T(8,128)(4,1)S(1)} %broadcast_compare_fusion, bf16[2048,1,128]{2,0,1:T(8,128)(2,1)S(1)} %copy-done.1, bf16[512,1024]{1,0:T(8,128)(2,1)} %all-gather.3.cloned.1.call-done), kind=kOutput, calls=%fused_computation.1 | convolution fusion | flops 2172645376 | bytes 36192256 | tf_op jit(solution)/shard_map/rgd,td->rgt/dot_general | solution.py:67
  162.5 72.1 %pmax.7 = f32[512,8]{0,1:T(8,128)S(1)} all-reduce(f32[512,8]{0,1:T(8,128)S(1)} %max.5), channel_id=1, replica_groups=mesh['sec'=2,'head'=4,'ctx'=16] {'ctx'}, use_global_device_ids=true, to_apply=%region_4.5 | all-reduce | flops 4096 | bytes 32768 | tf_op jit(solution)/shard_map/pmax | solution.py:76
  234.6 15.2 %fusion = f32[512,8]{0,1:T(8,128)S(1)} fusion(f32[512,8,2048]{2,0,1:T(8,128)} %get-tuple-element.6, f32[512,8]{0,1:T(8,128)S(1)} %pmax.7, pred[512,2048]{1,0:T(8,128)(4,1)S(1)} %broadcast_compare_fusion), kind=kLoop, calls=%fused_computation.2 | loop fusion | flops 33550336 | bytes 34635776 | tf_op jit(solution)/shard_map/reduce_sum | solution.py:79
  249.8 15.4 %fusion.2 = f32[512,8,128]{0,2,1:T(8,128)} fusion(f32[512,8,2048]{2,0,1:T(8,128)} %get-tuple-element.6, f32[512,8]{0,1:T(8,128)S(1)} %pmax.7, pred[512,2048]{1,0:T(8,128)(4,1)S(1)} %broadcast_compare_fusion, bf16[2048,1,128]{2,0,1:T(8,128)(2,1)} %param.17), kind=kOutput, calls=%fused_computation.4 | convolution fusion | flops 2181038080 | bytes 37240832 | tf_op jit(solution)/shard_map/rgt,td->rgd/dot_general | solution.py:80
  265.3 2.1 convolution_add_fusion
  267.7 2.0 copy.25
  269.7 72.2 %reduce-scatter.10.cloned.1.call-done = f32[32,1152]{1,0:T(8,128)} async-done(((f32[512,1152]{1,0:T(8,128)}), f32[32,1152]{1,0:T(8,128)}) %reduce-scatter.10.cloned.1.call-update) | async-done | bytes 147472
  341.9 0.9 slice.36
  343.0 0.7 slice.37
  343.8 0.8 copy.21
  344.7 42.0 %all-gather.5.cloned.1.call-done = bf16[512,1024]{1,0:T(8,128)(2,1)} async-done(((bf16[32,1024]{1,0:T(8,128)(2,1)}), bf16[512,1024]{1,0:T(8,128)(2,1)}) %all-gather.5.cloned.1.call-update) | async-done | bytes 1048592 | tf_op jit(solution)/shard_map/all_gather | solution.py:101
  386.6 2.8 convolution_convert_fusion
  389.4 30.6 %reduce-scatter.8.cloned.1.call-done = bf16[64,512]{1,0:T(8,128)(2,1)} async-done(((bf16[512,512]{1,0:T(8,128)(2,1)}), bf16[64,512]{1,0:T(8,128)(2,1)}) %reduce-scatter.8.cloned.1.call-update) | async-done | bytes 65552 | tf_op jit(solution)/shard_map/reduce_scatter | solution.py:102
  (36 shorter events, 3.2 us)
Async XLA Ops:
  6.5 380.1 %copy-start = (bf16[1024,512]{1,0:T(8,128)(2,1)S(1)}, bf16[1024,512]{1,0:T(8,128)(2,1)}, u32[]{:S(2)}) copy-start(bf16[1024,512]{1,0:T(8,128)(2,1)} %param.15) | copy-start | bytes 3145732
  6.5 94.7 %reduce-scatter.6.cloned.1.call-start = ((), (), s32[]{:S(2)}) async-start(), calls=%async_computation.3 | async-start | bytes 3063808 | tf_op jit(solution)/shard_map/reduce_scatter | solution.py:50
  22.1 81.8 %copy-start.2 = (s32[32]{0:T(128)S(1)}, s32[32]{0:T(128)}, u32[]{:S(2)}) copy-start(s32[32]{0:T(128)} %param.18) | copy-start | bytes 388
  22.1 82.0 %copy-start.3 = (s32[512]{0:T(512)S(1)}, s32[512]{0:T(512)}, u32[]{:S(2)}) copy-start(s32[512]{0:T(512)} %param.19) | copy-start | bytes 6148
  22.1 123.6 %all-gather.3.cloned.1.call-start = ((), (), s32[]{:S(2)}) async-start(), calls=%async_computation.4 | async-start | bytes 1114112 | tf_op jit(solution)/shard_map/all_gather | solution.py:57
  103.8 238.1 %reduce-scatter.10.cloned.1.call-start = ((), (), s32[]{:S(2)}) async-start(), calls=%async_computation.7 | async-start | bytes 2506752
  104.7 42.7 %copy-start.1 = (bf16[2048,1,128]{2,0,1:T(8,128)(2,1)S(1)}, bf16[2048,1,128]{2,0,1:T(8,128)(2,1)}, u32[]{:S(2)}) copy-start(bf16[2048,1,128]{2,0,1:T(8,128)(2,1)} %param.16) | copy-start | bytes 1572868
  269.7 117.0 %all-gather.5.cloned.1.call-start = ((), (), s32[]{:S(2)}) async-start(), calls=%async_computation.5 | async-start | bytes 1114112 | tf_op jit(solution)/shard_map/all_gather | solution.py:101
  344.6 75.4 %reduce-scatter.8.cloned.1.call-start = ((), (), s32[]{:S(2)}) async-start(), calls=%async_computation.6 | async-start | bytes 589824 | tf_op jit(solution)/shard_map/reduce_scatter | solution.py:102
Sparse Core Ops, SparseCore 0:
  22.2 79.0 reduce-scatter.5
  103.9 41.7 all-gather.2
  269.8 72.0 reduce-scatter.9
  344.7 41.8 all-gather.4
  389.5 30.4 reduce-scatter.7
where the time goes:
time: 427 us
  waiting for transfers between devices  263 us (62%)
  blocking collectives  82.6 us (19%)
  matrix products  41.4 us (10%)
  other arithmetic  20.8 us (5%)
  between operations  13.3 us (3%)
  local copies, waits for them, and re-layouts  5.52 us (1%)
    reduce_scatter x1, waiting for transfers between devices, body(): reduced = lax.psum_scatter(packed, 'ctx', scatter_dimension=0, tiled=True)  79.1 us
    unnamed x6, waiting for transfers between devices  72.2 us
    pmax x1, blocking collectives, body(): highest = lax.pmax(local_high, 'ctx')  72.1 us
    all_gather x1, waiting for transfers between devices, body(): attended = lax.all_gather(own_attended, 'ctx', axis=0, tiled=True)  42 us
    all_gather x1, waiting for transfers between devices, body(): queries = lax.all_gather(own_queries, 'ctx', axis=0, tiled=True)  38.8 us
    reduce_scatter x1, waiting for transfers between devices, body(): lax.psum_scatter(jnp.dot(attended, out_weight, preferred_element_type=jnp...  30.6 us
    dot_general x1, matrix products, body(): jnp.einsum('rgt,td->rgd', weights.astype(jnp.bfloat16), vals, preferred_e...  15.4 us
    reduce_sum x2, other arithmetic, body(): weight_sum = jnp.sum(weights, axis=2) + jnp.sum(tree_weights, axis=2)  15.3 us
  transfers between devices with their start and end apart: 5, of which 5 were waited for; matrix products, arithmetic and copies ran while one was open for 1% of the time, Pallas kernels for 0%

commit v1 on v0

--- a/solution.py
+++ b/solution.py
@@ -98,7 +98,11 @@
         .reshape(row_share, query_width)
         .astype(jnp.bfloat16)
     )
-    attended = lax.all_gather(own_attended, "ctx", axis=0, tiled=True)
+    length = lax.axis_size("ctx")
+    repeats = [length if d == 0 else 1 for d in range(own_attended.ndim)]
+    attended = lax.all_to_all(
+        jnp.tile(own_attended, repeats), "ctx", split_axis=0, concat_axis=0, tiled=True
+    )
     return lax.psum_scatter(
         jnp.dot(attended, out_weight, preferred_element_type=jnp.float32).astype(jnp.bfloat16),
         ("sec", "head"),

time: 427 us -> 402 us (0.941)
  waiting for transfers between devices: 263 us -> 219 us
  blocking collectives: 82.6 us -> 103 us
    all_gather x1 -> x0, waiting for transfers between devices: 42 us -> none  [body(): attended = lax.all_gather(own_attended, 'ctx', axis=0, tiled=True)]
    all_to_all x0 -> x1, blocking collectives: none -> 20.1 us  [body(): lax.all_to_all(jnp.tile(own_attended, repeats), 'ctx', split_axis=0, conc...]
    unnamed x6 -> x5, waiting for transfers between devices: 72.2 us -> 72.2 us
  transfers between devices with their start and end apart: 5 -> 4, of which waited for: 5 -> 4; matrix products, arithmetic and copies ran while one was open for 1% -> 1% of each run, Pallas kernels for 0% -> 0%
where the time goes in v1:
time: 402 us; the launch traced here: 401 us
  waiting for transfers between devices  219 us (54%)
  blocking collectives  103 us (26%)
  matrix products  40.2 us (10%)
  other arithmetic  20.8 us (5%)
  between operations  13.3 us (3%)
  local copies, waits for them, and re-layouts  5 us (1%)
    reduce_scatter x1, waiting for transfers between devices, body(): reduced = lax.psum_scatter(packed, 'ctx', scatter_dimension=0, tiled=True)  79.1 us
    unnamed x5, waiting for transfers between devices  72.2 us
    pmax x1, blocking collectives, body(): highest = lax.pmax(local_high, 'ctx')  72.1 us
    all_gather x1, waiting for transfers between devices, body(): queries = lax.all_gather(own_queries, 'ctx', axis=0, tiled=True)  38.8 us
    reduce_scatter x1, waiting for transfers between devices, body(): lax.psum_scatter(jnp.dot(attended, out_weight, preferred_element_type=jnp...  28.7 us
    all_to_all x1, blocking collectives, body(): lax.all_to_all(jnp.tile(own_attended, repeats), 'ctx', split_axis=0, conc...  20.1 us
    dot_general x1, matrix products, body(): jnp.einsum('rgt,td->rgd', weights.astype(jnp.bfloat16), vals, preferred_e...  15.4 us
    reduce_sum x2, other arithmetic, body(): weight_sum = jnp.sum(weights, axis=2) + jnp.sum(tree_weights, axis=2)  15.3 us
  transfers between devices with their start and end apart: 4, of which 4 were waited for; matrix products, arithmetic and copies ran while one was open for 1% of the time, Pallas kernels for 0%

profile of v1, /device:TPU:0, one launch (start us, length us, event | category | flops | bytes accessed | tf_op | source)
XLA Modules:
  0.0 400.9 jit_solution(6179837839018597343)
XLA Ops:
  6.5 10.5 %all_gather.6 = bf16[512,512]{1,0:T(8,128)(2,1)S(1)} all-gather(bf16[256,512]{1,0:T(8,128)(2,1)} %param.10), channel_id=1, replica_groups=mesh['sec'=2,'head'=4,'ctx'=16] {'sec'}, dimensions={0}, use_global_device_ids=true | all-gather | bytes 786432 | tf_op jit(solution)/shard_map/all_gather | solution.py:36
  17.0 0.7 convert_element_type.29
  18.0 2.2 fusion.5
  20.3 1.8 pad_maximum_fusion
  22.1 79.1 %reduce-scatter.6.cloned.1.call-done = f32[32,1408]{1,0:T(8,128)} async-done(((f32[512,1408]{1,0:T(8,128)}), f32[32,1408]{1,0:T(8,128)}) %reduce-scatter.6.cloned.1.call-update) | async-done | bytes 180240 | tf_op jit(solution)/shard_map/reduce_scatter | solution.py:50
  101.3 0.8 fusion.37
  102.1 1.0 fusion.34
  104.1 0.6 convolution_compare_fusion.2
  104.7 1.1 convolution_compare_fusion
  106.3 0.7 broadcast_compare_fusion
  106.9 38.8 %all-gather.2.cloned.1.call-done = bf16[512,1024]{1,0:T(8,128)(2,1)} async-done(((bf16[32,1024]{1,0:T(8,128)(2,1)}), bf16[512,1024]{1,0:T(8,128)(2,1)}) %all-gather.2.cloned.1.call-update) | async-done | bytes 1048592 | tf_op jit(solution)/shard_map/all_gather | solution.py:57
  145.7 1.7 select_reduce_fusion.1
  147.4 15.1 %select_reduce_fusion = (f32[512,8]{0,1:T(8,128)S(1)}, f32[512,8,2048]{2,0,1:T(8,128)}) fusion(pred[512,2048]{1,0:T(8,128)(4,1)S(1)} %broadcast_compare_fusion, bf16[2048,1,128]{2,0,1:T(8,128)(2,1)S(1)} %copy-done.1, bf16[512,1024]{1,0:T(8,128)(2,1)} %all-gather.2.cloned.1.call-done), kind=kOutput, calls=%fused_computation.1 | convolution fusion | flops 2172645376 | bytes 36192256 | tf_op jit(solution)/shard_map/rgd,td->rgt/dot_general | solution.py:67
  162.5 72.1 %pmax.7 = f32[512,8]{0,1:T(8,128)S(1)} all-reduce(f32[512,8]{0,1:T(8,128)S(1)} %max.5), channel_id=1, replica_groups=mesh['sec'=2,'head'=4,'ctx'=16] {'ctx'}, use_global_device_ids=true, to_apply=%region_4.5 | all-reduce | flops 4096 | bytes 32768 | tf_op jit(solution)/shard_map/pmax | solution.py:76
  234.6 15.2 %fusion = f32[512,8]{0,1:T(8,128)S(1)} fusion(f32[512,8,2048]{2,0,1:T(8,128)} %get-tuple-element.6, f32[512,8]{0,1:T(8,128)S(1)} %pmax.7, pred[512,2048]{1,0:T(8,128)(4,1)S(1)} %broadcast_compare_fusion), kind=kLoop, calls=%fused_computation.2 | loop fusion | flops 33550336 | bytes 34635776 | tf_op jit(solution)/shard_map/reduce_sum | solution.py:79
  249.8 15.4 %fusion.2 = f32[512,8,128]{0,2,1:T(8,128)} fusion(f32[512,8,2048]{2,0,1:T(8,128)} %get-tuple-element.6, f32[512,8]{0,1:T(8,128)S(1)} %pmax.7, pred[512,2048]{1,0:T(8,128)(4,1)S(1)} %broadcast_compare_fusion, bf16[2048,1,128]{2,0,1:T(8,128)(2,1)} %param.17), kind=kOutput, calls=%fused_computation.4 | convolution fusion | flops 2181038080 | bytes 37240832 | tf_op jit(solution)/shard_map/rgt,td->rgd/dot_general | solution.py:80
  265.3 2.1 convolution_add_fusion
  267.7 2.0 copy.27
  269.7 72.2 %reduce-scatter.10.cloned.1.call-done = f32[32,1152]{1,0:T(8,128)} async-done(((f32[512,1152]{1,0:T(8,128)}), f32[32,1152]{1,0:T(8,128)}) %reduce-scatter.10.cloned.1.call-update) | async-done | bytes 147472
  341.9 0.9 slice.36
  343.0 0.7 slice.37
  344.1 20.1 %all_to_all.9 = bf16[16,32,1024]{2,1,0:T(8,128)(2,1)S(1)} all-to-all(bf16[16,32,1024]{2,1,0:T(8,128)(2,1)S(1)} %tile.2), channel_id=1, replica_groups=mesh['sec'=2,'head'=4,'ctx'=16] {'ctx'}, dimensions={0} | all-to-all | bytes 2097152 | tf_op jit(solution)/shard_map/all_to_all | solution.py:103
  364.2 1.5 convolution_convert_fusion
  365.7 28.7 %reduce-scatter.8.cloned.1.call-done = bf16[64,512]{1,0:T(8,128)(2,1)} async-done(((bf16[512,512]{1,0:T(8,128)(2,1)}), bf16[64,512]{1,0:T(8,128)(2,1)}) %reduce-scatter.8.cloned.1.call-update) | async-done | bytes 65552 | tf_op jit(solution)/shard_map/reduce_scatter | solution.py:106
  (35 shorter events, 2.7 us)
Async XLA Ops:
  6.5 357.6 %copy-start = (bf16[1024,512]{1,0:T(8,128)(2,1)S(1)}, bf16[1024,512]{1,0:T(8,128)(2,1)}, u32[]{:S(2)}) copy-start(bf16[1024,512]{1,0:T(8,128)(2,1)} %param.15) | copy-start | bytes 3145732
  6.5 94.7 %reduce-scatter.6.cloned.1.call-start = ((), (), s32[]{:S(2)}) async-start(), calls=%async_computation.4 | async-start | bytes 3063808 | tf_op jit(solution)/shard_map/reduce_scatter | solution.py:50
  22.1 81.8 %copy-start.2 = (s32[32]{0:T(128)S(1)}, s32[32]{0:T(128)}, u32[]{:S(2)}) copy-start(s32[32]{0:T(128)} %param.18) | copy-start | bytes 388
  22.1 82.0 %copy-start.3 = (s32[512]{0:T(512)S(1)}, s32[512]{0:T(512)}, u32[]{:S(2)}) copy-start(s32[512]{0:T(512)} %param.19) | copy-start | bytes 6148
  22.1 123.6 %all-gather.2.cloned.1.call-start = ((), (), s32[]{:S(2)}) async-start(), calls=%async_computation.5 | async-start | bytes 1114112 | tf_op jit(solution)/shard_map/all_gather | solution.py:57
  103.8 238.1 %reduce-scatter.10.cloned.1.call-start = ((), (), s32[]{:S(2)}) async-start(), calls=%async_computation.7 | async-start | bytes 2506752
  104.7 42.7 %copy-start.1 = (bf16[2048,1,128]{2,0,1:T(8,128)(2,1)S(1)}, bf16[2048,1,128]{2,0,1:T(8,128)(2,1)}, u32[]{:S(2)}) copy-start(bf16[2048,1,128]{2,0,1:T(8,128)(2,1)} %param.16) | copy-start | bytes 1572868
  269.7 124.7 %reduce-scatter.8.cloned.1.call-start = ((), (), s32[]{:S(2)}) async-start(), calls=%async_computation.6 | async-start | bytes 589824 | tf_op jit(solution)/shard_map/reduce_scatter | solution.py:106
Sparse Core Ops, SparseCore 0:
  22.2 79.0 reduce-scatter.5
  103.9 41.7 all-gather.1
  269.8 72.0 reduce-scatter.9
  365.8 28.5 reduce-scatter.7
